TPU v7x, 256 devices: a whole 4x4x8 slice. The times are simulated.
256 devices in a mesh: dp: 32 (over x_lo, z, core), tensor: 8 (over x_hi, y).
Axes of the slice: x: 4 (x_hi: 2, x_lo: 2; x = x_hi * 2 + x_lo), y: 4, z: 8, core: 2. Of those that a mesh axis runs over, the one named last changes fastest.
Arguments:
- hidden_input_state: bfloat16 [12288, 4608], P('dp', 'tensor'), may hold values from -80 to 80
- norm_gain: float32 [4608], replicated, may hold values from 0.5 to 1.5
- head_weight: bfloat16 [4608, 8192], P(None, 'tensor'), may hold values from -2 to 2
- target_ids: int32 [12288], P('dp'), may hold values from 0 to 8191
Outputs:
- hidden_state_gradient: float32 [12288, 4608], P('dp', 'tensor')
- grad_head: float32 [4608, 8192], P('dp', 'tensor')
- norm_gain_gradient: float32 [4608], P('tensor')
All inputs are finite; a program needn't handle non-finite values.
Results may differ from a plain program's by a relative error of at most 0.0039.
Values may be sent and summed in bfloat16 or wider, within the bound.
No kernel may reach another device: no remote copies, remote signals or barrier semaphores. Data moves between devices by JAX's collectives and lax.ppermute only.
A program may use at most 192 MiB of HBM per device.

v0:
```python
import jax
import jax.numpy as jnp
import numpy as np
from jax import lax
from jax.sharding import PartitionSpec as P

epsilon = 1e-06


def ring_order(n_hi, n_lo):
    order = []
    for hi in range(n_hi):
        los = range(n_lo) if hi % 2 == 0 else range(n_lo - 1, -1, -1)
        order += [hi * n_lo + lo for lo in los]
    return order


def ring_reduce_scatter(fwd, bwd, axis, order):
    n = len(order)
    pos_of = np.zeros(n, np.int32)
    for p, t in enumerate(order):
        pos_of[t] = p
    order_arr = jnp.asarray(np.asarray(order, np.int32))
    me = lax.axis_index(axis)
    pos = jnp.asarray(pos_of)[me]
    perm_f = [(order[p], order[(p + 1) % n]) for p in range(n)]
    perm_b = [(order[p], order[(p - 1) % n]) for p in range(n)]
    recv_f = recv_b = None
    for s in range(n - 1):
        qf = order_arr[(pos - 1 - s) % n]
        qb = order_arr[(pos + 1 + s) % n]
        send_f = lax.dynamic_index_in_dim(fwd, qf, 0, keepdims=False)
        send_b = lax.dynamic_index_in_dim(bwd, qb, 0, keepdims=False)
        if recv_f is not None:
            send_f = send_f + recv_f
            send_b = send_b + recv_b
        recv_f = lax.ppermute(send_f, axis, perm_f)
        recv_b = lax.ppermute(send_b, axis, perm_b)
    own_f = lax.dynamic_index_in_dim(fwd, me, 0, keepdims=False)
    own_b = lax.dynamic_index_in_dim(bwd, me, 0, keepdims=False)
    return (own_f + recv_f, own_b + recv_b)


def shards(hidden_input_state, norm_gain, head_weight, target_ids):
    tokens, local_cols = hidden_input_state.shape
    width, vocab_rows = head_weight.shape
    n_tensor = width // local_cols
    gathered = lax.all_gather(hidden_input_state, "tensor", axis=1, tiled=True)
    values = gathered.astype(jnp.float32)
    scaled_rows = lax.rsqrt(jnp.mean(values * values, axis=1, keepdims=True) + epsilon)
    normalized = values * scaled_rows
    normed = (normalized * norm_gain[None, :]).astype(jnp.bfloat16)
    logits = jnp.dot(normed, head_weight, preferred_element_type=jnp.float32)
    local_top = jnp.max(logits, axis=1)
    local_total = jnp.sum(jnp.exp(logits - local_top[:, None]), axis=1)
    stats = lax.all_gather(jnp.stack([local_top, local_total]), "tensor", axis=0)
    row_top = jnp.max(stats[:, 0, :], axis=0)
    row_total = jnp.sum(stats[:, 1, :] * jnp.exp(stats[:, 0, :] - row_top[None, :]), axis=0)
    log_total = row_top + jnp.log(row_total)
    offset = lax.axis_index("tensor") * vocab_rows
    column_ids = offset + lax.broadcasted_iota(jnp.int32, (1, vocab_rows), 1)
    onehot = (column_ids == target_ids[:, None]).astype(jnp.float32)
    dlogits = (jnp.exp(logits - log_total[:, None]) - onehot).astype(jnp.bfloat16)
    grad_head = lax.psum_scatter(
        lax.dot_general(
            normed, dlogits, (((0,), (0,)), ((), ())), preferred_element_type=jnp.float32
        ),
        "dp",
        scatter_dimension=0,
        tiled=True,
    )
    partial = lax.dot_general(
        head_weight, dlogits, (((1,), (1,)), ((), ())), preferred_element_type=jnp.float32
    )
    inner_part = jnp.sum(partial * (norm_gain[:, None] * normalized.T), axis=0)
    chunks = partial.reshape(n_tensor, local_cols, tokens)
    half = local_cols // 2
    extra = (
        jnp.zeros((n_tensor, 8, tokens), jnp.float32)
        .at[:, 0, :]
        .set(jnp.broadcast_to(inner_part[None, :], (n_tensor, tokens)))
    )
    fwd = jnp.concatenate([chunks[:, :half, :], extra], axis=1)
    bwd = chunks[:, half:, :]
    order = ring_order(2, n_tensor // 2)
    got_f, got_b = ring_reduce_scatter(fwd, bwd, "tensor", order)
    grad_cols = jnp.concatenate([got_f[:half], got_b], axis=0)
    row_inner_sum = got_f[half] / width
    normed_gradient = grad_cols.T
    start_col = lax.axis_index("tensor") * local_cols
    normalized_slice = hidden_input_state.astype(jnp.float32) * scaled_rows
    gain_slice = lax.dynamic_slice_in_dim(norm_gain, start_col, local_cols)
    weighted_rows = normed_gradient * gain_slice[None, :]
    hidden_state_gradient = scaled_rows * (
        weighted_rows - normalized_slice * row_inner_sum[:, None]
    )
    norm_gain_gradient = lax.psum(jnp.sum(normed_gradient * normalized_slice, axis=0), "dp")
    return (hidden_state_gradient, grad_head, norm_gain_gradient)


def solution(mesh):
    return jax.shard_map(
        shards,
        mesh=mesh,
        in_specs=(P("dp", "tensor"), P(), P(None, "tensor"), P("dp")),
        out_specs=(P("dp", "tensor"), P("dp", "tensor"), P("tensor")),
        check_vma=False,
    )
```

profile of v0, /device:TPU:1, one launch (start us, length us, event | category | flops | bytes accessed | tf_op | source)
XLA Modules:
  0.0 408.9 jit_solution(1212143429641370767)
XLA Ops:
  8.0 77.0 %all-gather.4.cloned.1.call-done = bf16[384,4608]{0,1:T(8,128)(2,1)} async-done(((bf16[384,576]{0,1:T(8,128)(2,1)}), bf16[384,4608]{0,1:T(8,128)(2,1)}) %all-gather.4.cloned.1.call-update) | async-done | bytes 3538960 | tf_op jit(solution)/shard_map/all_gather | solution.py:48
  85.0 4.3 %copy.30 = bf16[384,4608]{1,0:T(8,128)(2,1)S(1)} copy(bf16[384,4608]{0,1:T(8,128)(2,1)} %all-gather.4.cloned.1.call-done) | data formatting | bytes 7077888 | tf_op jit(solution)/shard_map/all_gather | solution.py:48
  90.1 6.6 %fusion.17 = (f32[384]{0:T(512)S(1)}, f32[384,1024]{1,0:T(8,128)S(1)}) fusion(bf16[4608,1024]{1,0:T(8,128)(2,1)} %param.10, bf16[384,4608]{1,0:T(8,128)(2,1)S(1)} %copy.30, f32[4608]{0:T(1024)S(1)} %copy-done.6, f32[384]{0:T(512)S(1)} %add_rsqrt_fusion), kind=kOutput, calls=%fused_computation.50 | convolution fusion | flops 3631349248 | bytes 14570496 | tf_op jit(solution)/shard_map/dot_general | solution.py:53
  97.2 27.8 %all-gather.1 = f32[8,2,384]{2,1,0:T(2,128)S(1)} all-gather(f32[1,2,384]{2,1,0:T(2,128)S(1)} %maximum_bitcast_fusion.1), channel_id=2, replica_groups=mesh['dp'=32,'tensor'=8] {'tensor'}, dimensions={0}, use_global_device_ids=true | all-gather | bytes 27648 | tf_op jit(solution)/shard_map/all_gather | solution.py:56
  125.1 9.5 %fusion.6 = f32[4608,1024]{1,0:T(8,128)} fusion(bf16[384,4608]{1,0:T(8,128)(2,1)S(1)} %copy.30, f32[4608]{0:T(1024)S(1)} %copy-done.6, f32[384]{0:T(512)S(1)} %add_rsqrt_fusion, f32[384,1024]{1,0:T(8,128)S(1)} %get-tuple-element.37, s32[1024]{0:T(1024)S(1)} %iota_add_fusion, f32[384]{0:T(512)S(1)} %log_add_fusion, s32[384]{0:T(512)S(1)} %copy-done.7), kind=kOutput, calls=%fused_computation.13 | convolution fusion | flops 3632922624 | bytes 24013312 | tf_op jit(solution)/shard_map/dot_general | solution.py:65
  149.5 11.5 %fusion.5 = (f32[384]{0:T(512)S(1)}, f32[4608,384]{0,1:T(8,128)}) fusion(bf16[384,4608]{1,0:T(8,128)(2,1)S(1)} %copy.30, f32[4608]{0:T(1024)} %param.9, f32[384]{0:T(512)S(1)} %add_rsqrt_fusion, bf16[4608,1024]{1,0:T(8,128)(2,1)} %param.10, f32[384,1024]{1,0:T(8,128)} %copy-done.3, s32[1024]{0:T(1024)S(1)} %iota_add_fusion, f32[384]{0:T(512)S(1)} %log_add_fusion, ...), kind=kOutput, calls=%fused_computation.8 | convolution fusion | flops 3634691584 | bytes 21655552 | tf_op jit(solution)/shard_map/dot_general | solution.py:72
  161.0 8.1 %copy.32 = f32[4608,384]{1,0:T(8,128)} copy(f32[4608,384]{0,1:T(8,128)} %get-tuple-element.39) | data formatting | bytes 14155776 | tf_op jit(solution)/shard_map/dot_general | solution.py:72
  169.1 3.7 fusion.14
  182.4 16.3 %collective-permute-done.7 = f32[288,384]{1,0:T(8,128)} collective-permute-done((f32[288,384]{1,0:T(8,128)}, f32[288,384]{1,0:T(8,128)}, u32[]{:S(2)}, u32[]{:S(2)}) %collective-permute-start.7) | collective-permute-done | bytes 442400 | tf_op jit(solution)/shard_map/ppermute | solution.py:38
  200.7 7.0 %collective-permute-start.8 = (f32[288,384]{1,0:T(8,128)}, f32[288,384]{1,0:T(8,128)}, u32[]{:S(2)}, u32[]{:S(2)}) collective-permute-start(f32[288,384]{1,0:T(8,128)} %bitcast_add_fusion.7), channel_id=1, source_target_pairs={{0,4},{1,0},{2,1},{3,2},{7,3},{6,7},{5,6},{4,5},{8,12},{9,8},{10,9... | collective-permute-start | bytes 1327112 | tf_op jit(solution)/shard_map/ppermute | solution.py:38
  207.7 7.3 %collective-permute-done = f32[296,384]{1,0:T(8,128)} collective-permute-done((f32[296,384]{1,0:T(8,128)}, f32[296,384]{1,0:T(8,128)}, u32[]{:S(2)}, u32[]{:S(2)}) %collective-permute-start) | collective-permute-done | bytes 454688 | tf_op jit(solution)/shard_map/ppermute | solution.py:37
  220.7 10.4 %collective-permute-done.8 = f32[288,384]{1,0:T(8,128)} collective-permute-done((f32[288,384]{1,0:T(8,128)}, f32[288,384]{1,0:T(8,128)}, u32[]{:S(2)}, u32[]{:S(2)}) %collective-permute-start.8) | collective-permute-done | bytes 442400 | tf_op jit(solution)/shard_map/ppermute | solution.py:38
  233.1 6.2 %collective-permute-start.9 = (f32[288,384]{1,0:T(8,128)}, f32[288,384]{1,0:T(8,128)}, u32[]{:S(2)}, u32[]{:S(2)}) collective-permute-start(f32[288,384]{1,0:T(8,128)} %bitcast_add_fusion.8), channel_id=1, source_target_pairs={{0,4},{1,0},{2,1},{3,2},{7,3},{6,7},{5,6},{4,5},{8,12},{9,8},{10,9... | collective-permute-start | bytes 1327112 | tf_op jit(solution)/shard_map/ppermute | solution.py:38
  239.3 10.3 %collective-permute-done.1 = f32[296,384]{1,0:T(8,128)} collective-permute-done((f32[296,384]{1,0:T(8,128)}, f32[296,384]{1,0:T(8,128)}, u32[]{:S(2)}, u32[]{:S(2)}) %collective-permute-start.1) | collective-permute-done | bytes 454688 | tf_op jit(solution)/shard_map/ppermute | solution.py:37
  255.1 18.2 %collective-permute-done.9 = f32[288,384]{1,0:T(8,128)} collective-permute-done((f32[288,384]{1,0:T(8,128)}, f32[288,384]{1,0:T(8,128)}, u32[]{:S(2)}, u32[]{:S(2)}) %collective-permute-start.9) | collective-permute-done | bytes 442400 | tf_op jit(solution)/shard_map/ppermute | solution.py:38
  275.2 3.8 collective-permute-start.10
  279.0 5.7 %collective-permute-done.2 = f32[296,384]{1,0:T(8,128)} collective-permute-done((f32[296,384]{1,0:T(8,128)}, f32[296,384]{1,0:T(8,128)}, u32[]{:S(2)}, u32[]{:S(2)}) %collective-permute-start.2) | collective-permute-done | bytes 454688 | tf_op jit(solution)/shard_map/ppermute | solution.py:37
  290.6 3.5 collective-permute-done.10
  295.9 3.7 collective-permute-start.11
  309.5 3.7 collective-permute-start.12
  322.2 3.7 collective-permute-start.13
  328.7 3.4 collective-permute-done.13
  333.1 4.5 %collective-permute-done.6 = f32[296,384]{1,0:T(8,128)} collective-permute-done((f32[296,384]{1,0:T(8,128)}, f32[296,384]{1,0:T(8,128)}, u32[]{:S(2)}, u32[]{:S(2)}) %collective-permute-start.6) | collective-permute-done | bytes 454688 | tf_op jit(solution)/shard_map/ppermute | solution.py:37
  340.0 62.0 %psum.7 = f32[576]{0:T(1024)} all-reduce(f32[576]{0:T(1024)S(1)} %get-tuple-element.17), channel_id=1, replica_groups=mesh['dp'=32,'tensor'=8] {'dp'}, use_global_device_ids=true, to_apply=%region_8.9 | all-reduce | flops 576 | bytes 4608 | tf_op jit(solution)/shard_map/psum | solution.py:97
  (68 shorter events, 40.5 us)
Async XLA Ops:
  7.2 77.8 %all-gather.4.cloned.1.call-start = ((), (), s32[]{:S(2)}) async-start(), calls=%async_computation.1 | async-start | bytes 3981312 | tf_op jit(solution)/shard_map/all_gather | solution.py:48
  7.9 394.1 %reduce-scatter.2.cloned.1.call-start = ((), (), s32[]{:S(2)}) async-start(), calls=%async_computation.2 | async-start | bytes 19464192 | tf_op jit(solution)/shard_map/reduce_scatter | solution.py:64
  89.3 0.8 copy-start.6
  90.1 35.0 %copy-start.7 = (s32[384]{0:T(512)S(1)}, s32[384]{0:T(512)}, u32[]{:S(2)}) copy-start(s32[384]{0:T(512)} %param.11) | copy-start | bytes 4612
  96.8 28.3 %copy-start.3 = (f32[384,1024]{1,0:T(8,128)}, f32[384,1024]{1,0:T(8,128)S(1)}, u32[]{:S(2)}) copy-start(f32[384,1024]{1,0:T(8,128)S(1)} %get-tuple-element.37) | copy-start | bytes 4718596
  134.6 0.7 copy-start.5
  172.8 1.9 copy-start.1
  173.7 25.0 %collective-permute-start.7 = (f32[288,384]{1,0:T(8,128)}, f32[288,384]{1,0:T(8,128)}, u32[]{:S(2)}, u32[]{:S(2)}) collective-permute-start(f32[288,384]{1,0:T(8,128)} %dynamic-slice_bitcast_fusion.1), channel_id=1, source_target_pairs={{0,4},{1,0},{2,1},{3,2},{7,3},{6,7},{5,6},{4,5},{8,12},{9,8},{10,9... | collective-permute-start | bytes 1327112 | tf_op jit(solution)/shard_map/ppermute | solution.py:38
  174.7 1.9 copy-start
  177.4 96.0 %copy-start.2 = (f32[8,288,384]{2,1,0:T(8,128)S(1)}, f32[8,288,384]{2,1,0:T(8,128)}, u32[]{:S(2)}) copy-start(f32[8,288,384]{2,1,0:T(8,128)} %copy-done.1) | copy-start | bytes 10616836
  177.4 37.6 %collective-permute-start = (f32[296,384]{1,0:T(8,128)}, f32[296,384]{1,0:T(8,128)}, u32[]{:S(2)}, u32[]{:S(2)}) collective-permute-start(f32[296,384]{1,0:T(8,128)} %dynamic-slice_bitcast_fusion), channel_id=1, source_target_pairs={{0,1},{1,2},{2,3},{3,7},{7,6},{6,5},{5,4},{4,0},{8,9},{9,10},{10,1... | collective-permute-start | bytes 1363976 | tf_op jit(solution)/shard_map/ppermute | solution.py:37
  200.7 30.4 %collective-permute-start.8 = (f32[288,384]{1,0:T(8,128)}, f32[288,384]{1,0:T(8,128)}, u32[]{:S(2)}, u32[]{:S(2)}) collective-permute-start(f32[288,384]{1,0:T(8,128)} %bitcast_add_fusion.7), channel_id=1, source_target_pairs={{0,4},{1,0},{2,1},{3,2},{7,3},{6,7},{5,6},{4,5},{8,12},{9,8},{10,9... | collective-permute-start | bytes 1327112 | tf_op jit(solution)/shard_map/ppermute | solution.py:38
  217.0 32.6 %collective-permute-start.1 = (f32[296,384]{1,0:T(8,128)}, f32[296,384]{1,0:T(8,128)}, u32[]{:S(2)}, u32[]{:S(2)}) collective-permute-start(f32[296,384]{1,0:T(8,128)} %bitcast_add_fusion), channel_id=1, source_target_pairs={{0,1},{1,2},{2,3},{3,7},{7,6},{6,5},{5,4},{4,0},{8,9},{9,10},{10,1... | collective-permute-start | bytes 1363976 | tf_op jit(solution)/shard_map/ppermute | solution.py:37
  233.1 40.3 %collective-permute-start.9 = (f32[288,384]{1,0:T(8,128)}, f32[288,384]{1,0:T(8,128)}, u32[]{:S(2)}, u32[]{:S(2)}) collective-permute-start(f32[288,384]{1,0:T(8,128)} %bitcast_add_fusion.8), channel_id=1, source_target_pairs={{0,4},{1,0},{2,1},{3,2},{7,3},{6,7},{5,6},{4,5},{8,12},{9,8},{10,9... | collective-permute-start | bytes 1327112 | tf_op jit(solution)/shard_map/ppermute | solution.py:38
  251.6 33.1 %collective-permute-start.2 = (f32[296,384]{1,0:T(8,128)}, f32[296,384]{1,0:T(8,128)}, u32[]{:S(2)}, u32[]{:S(2)}) collective-permute-start(f32[296,384]{1,0:T(8,128)} %bitcast_add_fusion.1), channel_id=1, source_target_pairs={{0,1},{1,2},{2,3},{3,7},{7,6},{6,5},{5,4},{4,0},{8,9},{9,10},{10,1... | collective-permute-start | bytes 1363976 | tf_op jit(solution)/shard_map/ppermute | solution.py:37
  275.2 18.9 %collective-permute-start.10 = (f32[288,384]{1,0:T(8,128)}, f32[288,384]{1,0:T(8,128)}, u32[]{:S(2)}, u32[]{:S(2)}) collective-permute-start(f32[288,384]{1,0:T(8,128)} %bitcast_add_fusion.9), channel_id=1, source_target_pairs={{0,4},{1,0},{2,1},{3,2},{7,3},{6,7},{5,6},{4,5},{8,12},{9,8},{10,9... | collective-permute-start | bytes 1327112 | tf_op jit(solution)/shard_map/ppermute | solution.py:38
  286.7 13.0 %collective-permute-start.3 = (f32[296,384]{1,0:T(8,128)}, f32[296,384]{1,0:T(8,128)}, u32[]{:S(2)}, u32[]{:S(2)}) collective-permute-start(f32[296,384]{1,0:T(8,128)} %bitcast_add_fusion.2), channel_id=1, source_target_pairs={{0,1},{1,2},{2,3},{3,7},{7,6},{6,5},{5,4},{4,0},{8,9},{9,10},{10,1... | collective-permute-start | bytes 1363976 | tf_op jit(solution)/shard_map/ppermute | solution.py:37
  295.9 11.7 %collective-permute-start.11 = (f32[288,384]{1,0:T(8,128)}, f32[288,384]{1,0:T(8,128)}, u32[]{:S(2)}, u32[]{:S(2)}) collective-permute-start(f32[288,384]{1,0:T(8,128)} %bitcast_add_fusion.10), channel_id=1, source_target_pairs={{0,4},{1,0},{2,1},{3,2},{7,3},{6,7},{5,6},{4,5},{8,12},{9,8},{10,9... | collective-permute-start | bytes 1327112 | tf_op jit(solution)/shard_map/ppermute | solution.py:38
  301.6 11.6 %collective-permute-start.4 = (f32[296,384]{1,0:T(8,128)}, f32[296,384]{1,0:T(8,128)}, u32[]{:S(2)}, u32[]{:S(2)}) collective-permute-start(f32[296,384]{1,0:T(8,128)} %bitcast_add_fusion.3), channel_id=1, source_target_pairs={{0,1},{1,2},{2,3},{3,7},{7,6},{6,5},{5,4},{4,0},{8,9},{9,10},{10,1... | collective-permute-start | bytes 1363976 | tf_op jit(solution)/shard_map/ppermute | solution.py:37
  309.5 10.8 %collective-permute-start.12 = (f32[288,384]{1,0:T(8,128)}, f32[288,384]{1,0:T(8,128)}, u32[]{:S(2)}, u32[]{:S(2)}) collective-permute-start(f32[288,384]{1,0:T(8,128)} %bitcast_add_fusion.11), channel_id=1, source_target_pairs={{0,4},{1,0},{2,1},{3,2},{7,3},{6,7},{5,6},{4,5},{8,12},{9,8},{10,9... | collective-permute-start | bytes 1327112 | tf_op jit(solution)/shard_map/ppermute | solution.py:38
  315.2 10.7 %collective-permute-start.5 = (f32[296,384]{1,0:T(8,128)}, f32[296,384]{1,0:T(8,128)}, u32[]{:S(2)}, u32[]{:S(2)}) collective-permute-start(f32[296,384]{1,0:T(8,128)} %bitcast_add_fusion.4), channel_id=1, source_target_pairs={{0,1},{1,2},{2,3},{3,7},{7,6},{6,5},{5,4},{4,0},{8,9},{9,10},{10,1... | collective-permute-start | bytes 1363976 | tf_op jit(solution)/shard_map/ppermute | solution.py:37
  322.2 9.9 %collective-permute-start.13 = (f32[288,384]{1,0:T(8,128)}, f32[288,384]{1,0:T(8,128)}, u32[]{:S(2)}, u32[]{:S(2)}) collective-permute-start(f32[288,384]{1,0:T(8,128)} %bitcast_add_fusion.12), channel_id=1, source_target_pairs={{0,4},{1,0},{2,1},{3,2},{7,3},{6,7},{5,6},{4,5},{8,12},{9,8},{10,9... | collective-permute-start | bytes 1327112 | tf_op jit(solution)/shard_map/ppermute | solution.py:38
  327.8 9.8 %collective-permute-start.6 = (f32[296,384]{1,0:T(8,128)}, f32[296,384]{1,0:T(8,128)}, u32[]{:S(2)}, u32[]{:S(2)}) collective-permute-start(f32[296,384]{1,0:T(8,128)} %bitcast_add_fusion.5), channel_id=1, source_target_pairs={{0,1},{1,2},{2,3},{3,7},{7,6},{6,5},{5,4},{4,0},{8,9},{9,10},{10,1... | collective-permute-start | bytes 1363976 | tf_op jit(solution)/shard_map/ppermute | solution.py:37
  327.8 11.0 %copy-start.4 = (bf16[384,576]{0,1:T(8,128)(2,1)S(1)}, bf16[384,576]{0,1:T(8,128)(2,1)}, u32[]{:S(2)}) copy-start(bf16[384,576]{0,1:T(8,128)(2,1)} %param.8) | copy-start | bytes 1327108
Sparse Core Ops, SparseCore 0:
  10.6 74.3 all-gather.3
  134.7 149.8 reduce-scatter.1
where the time goes:
time: 410 us; the launch traced here: 409 us
  waiting for transfers between devices  161 us (39%)
  blocking collectives  89.8 us (22%)
  between operations  50.1 us (12%)
  starting transfers between devices  29.3 us (7%)
  other arithmetic  28.1 us (7%)
  matrix products  27.6 us (7%)
  local copies, waits for them, and re-layouts  22.9 us (6%)
    all_gather x1, waiting for transfers between devices, shards(): gathered = lax.all_gather(hidden_input_state, 'tensor', axis=1, tiled=True)  77 us
    psum x1, blocking collectives, shards(): lax.psum(jnp.sum(normed_gradient * normalized_slice, axis=0), 'dp')  62 us
    ppermute x7, waiting for transfers between devices, ring_reduce_scatter(): recv_b = lax.ppermute(send_b, axis, perm_b)  55.6 us
    ppermute x7, starting transfers between devices, ring_reduce_scatter(): recv_b = lax.ppermute(send_b, axis, perm_b)  28.5 us
    all_gather x1, blocking collectives, shards(): lax.all_gather(jnp.stack([local_top, local_total]), 'tensor', axis=0)  27.8 us
    ppermute x7, waiting for transfers between devices, ring_reduce_scatter(): recv_f = lax.ppermute(send_f, axis, perm_f)  27.7 us
    add x6, other arithmetic, ring_reduce_scatter(): send_f = send_f + recv_f  11.8 us
    dot_general x1, matrix products, shards(): lax.dot_general(head_weight, dlogits, (((1,), (1,)), ((), ())), preferred...  11.5 us
  transfers between devices with their start and end apart: 16, of which 12 were waited for; matrix products, arithmetic and copies ran while one was open for 13% of the time, Pallas kernels for 0%

commit v1 on v0

--- a/solution.py
+++ b/solution.py
@@ -3,8 +3,13 @@
 import numpy as np
 from jax import lax
 from jax.sharding import PartitionSpec as P
+from jax.lax import all_gather
 
 epsilon = 1e-06
+
+
+def _raise_ratios(x_local, bus_axis):
+    return all_gather(x_local, bus_axis).sum(axis=0)
 
 
 def ring_order(n_hi, n_lo):
@@ -94,7 +99,7 @@
     hidden_state_gradient = scaled_rows * (
         weighted_rows - normalized_slice * row_inner_sum[:, None]
     )
-    norm_gain_gradient = lax.psum(jnp.sum(normed_gradient * normalized_slice, axis=0), "dp")
+    norm_gain_gradient = _raise_ratios(jnp.sum(normed_gradient * normalized_slice, axis=0), "dp")
     return (hidden_state_gradient, grad_head, norm_gain_gradient)
 
 

time: 410 us -> 611 us (1.49)
  waiting for transfers between devices: 161 us -> 436 us
  blocking collectives: 89.8 us -> 27.6 us
  starting transfers between devices: 29.3 us -> 11.4 us
    unnamed x2 -> x4, waiting for transfers between devices: 0.7 us -> 192 us
    reduce_scatter x1, waiting for transfers between devices: 0.01 us -> 148 us  [shards(): lax.psum_scatter(lax.dot_general(normed, dlogits, (((0,), (0,)), ((), ())...]
    psum x1 -> x0, blocking collectives: 62 us -> none  [shards(): lax.psum(jnp.sum(normed_gradient * normalized_slice, axis=0), 'dp')]
    ppermute x7, waiting for transfers between devices: 55.6 us -> 8.33 us  [ring_reduce_scatter(): recv_b = lax.ppermute(send_b, axis, perm_b)]
    ppermute x7, starting transfers between devices: 28.5 us -> 10.7 us  [ring_reduce_scatter(): recv_b = lax.ppermute(send_b, axis, perm_b)]
    all_gather x1, waiting for transfers between devices: 77 us -> 60.7 us  [shards(): gathered = lax.all_gather(hidden_input_state, 'tensor', axis=1, tiled=True)]
  transfers between devices with their start and end apart: 16 -> 17, of which waited for: 12 -> 15; matrix products, arithmetic and copies ran while one was open for 13% -> 7% of each run, Pallas kernels for 0% -> 0%
where the time goes in v1:
time: 611 us; the launch traced here: 608 us
  waiting for transfers between devices  436 us (71%)
  between operations  50.7 us (8%)
  other arithmetic  29.2 us (5%)
  local copies, waits for them, and re-layouts  27.6 us (5%)
  blocking collectives  27.6 us (5%)
  matrix products  24.7 us (4%)
  starting transfers between devices  11.4 us (2%)
    unnamed x4, waiting for transfers between devices  192 us
    reduce_scatter x1, waiting for transfers between devices, shards(): lax.psum_scatter(lax.dot_general(normed, dlogits, (((0,), (0,)), ((), ())...  148 us
    all_gather x1, waiting for transfers between devices, shards(): gathered = lax.all_gather(hidden_input_state, 'tensor', axis=1, tiled=True)  60.7 us
    all_gather x1, blocking collectives, shards(): lax.all_gather(jnp.stack([local_top, local_total]), 'tensor', axis=0)  27.6 us
    ppermute x7, waiting for transfers between devices, ring_reduce_scatter(): recv_f = lax.ppermute(send_f, axis, perm_f)  27.3 us
  transfers between devices with their start and end apart: 17, of which 15 were waited for; matrix products, arithmetic and copies ran while one was open for 7% of the time, Pallas kernels for 0%

profile of v1, /device:TPU:1, one launch (start us, length us, event | category | flops | bytes accessed | tf_op | source)
XLA Modules:
  0.0 607.5 jit_solution(16007585319517078657)
XLA Ops:
  24.3 60.7 %all-gather.5.cloned.1.call-done = bf16[384,4608]{0,1:T(8,128)(2,1)} async-done(((bf16[384,576]{0,1:T(8,128)(2,1)}), bf16[384,4608]{0,1:T(8,128)(2,1)}) %all-gather.5.cloned.1.call-update) | async-done | bytes 3538960 | tf_op jit(solution)/shard_map/all_gather | solution.py:53
  85.0 4.3 copy.33
  90.2 7.0 %fusion.17 = (f32[384]{0:T(512)S(1)}, f32[384,1024]{1,0:T(8,128)S(1)}) fusion(bf16[4608,1024]{1,0:T(8,128)(2,1)} %param.10, bf16[384,4608]{1,0:T(8,128)(2,1)S(1)} %copy.33, f32[4608]{0:T(1024)S(1)} %copy-done.4, f32[384]{0:T(512)S(1)} %add_rsqrt_fusion), kind=kOutput, calls=%fused_computation.50 | convolution fusion | flops 3631349248 | bytes 14570496 | tf_op jit(solution)/shard_map/dot_general | solution.py:58
  97.6 27.6 %all-gather.2 = f32[8,2,384]{2,1,0:T(2,128)S(1)} all-gather(f32[1,2,384]{2,1,0:T(2,128)S(1)} %maximum_bitcast_fusion.1), channel_id=2, replica_groups=mesh['dp'=32,'tensor'=8] {'tensor'}, dimensions={0}, use_global_device_ids=true | all-gather | bytes 27648 | tf_op jit(solution)/shard_map/all_gather | solution.py:61
  125.4 6.8 %fusion.5 = (f32[384]{0:T(512)S(1)}, f32[4608,384]{0,1:T(8,128)}) fusion(bf16[384,4608]{1,0:T(8,128)(2,1)S(1)} %copy.33, f32[4608]{0:T(1024)S(1)} %copy-done.4, f32[384]{0:T(512)S(1)} %add_rsqrt_fusion, bf16[4608,1024]{1,0:T(8,128)(2,1)S(1)} %bitcast.94, f32[384,1024]{1,0:T(8,128)S(1)} %get-tuple-element.37, s32[1024]{0:T(1024)S(1)} %iota_add_fusion, ...), kind=kOutput, calls=%fused_computation.8 | convolution fusion | flops 3634691584 | bytes 21655552 | tf_op jit(solution)/shard_map/dot_general | solution.py:77
  132.2 8.0 %copy.35 = f32[4608,384]{1,0:T(8,128)} copy(f32[4608,384]{0,1:T(8,128)} %get-tuple-element.39) | data formatting | bytes 14155776 | tf_op jit(solution)/shard_map/dot_general | solution.py:77
  140.2 3.6 fusion.14
  154.7 2.3 collective-permute-start.8
  157.4 2.0 bitcast_add_fusion
  170.2 2.0 bitcast_add_fusion.1
  176.1 2.1 collective-permute-done.9
  181.1 3.0 collective-permute-done.2
  184.1 2.0 bitcast_add_fusion.2
  189.7 2.4 collective-permute-done.10
  195.0 4.0 collective-permute-done.3
  199.0 2.0 bitcast_add_fusion.3
  210.0 5.1 collective-permute-done.4
  222.9 3.0 collective-permute-start.13
  225.9 4.5 collective-permute-done.5
  230.3 2.0 bitcast_add_fusion.5
  236.1 8.6 %collective-permute-done.6 = f32[296,384]{1,0:T(8,128)} collective-permute-done((f32[296,384]{1,0:T(8,128)}, f32[296,384]{1,0:T(8,128)}, u32[]{:S(2)}, u32[]{:S(2)}) %collective-permute-start.6) | collective-permute-done | bytes 454688 | tf_op jit(solution)/shard_map/ppermute | solution.py:42
  249.2 10.9 %fusion.6 = f32[4608,1024]{1,0:T(8,128)} fusion(bf16[384,4608]{1,0:T(8,128)(2,1)S(1)} %copy.33, f32[4608]{0:T(1024)} %param.9, f32[384]{0:T(512)S(1)} %add_rsqrt_fusion, f32[384,1024]{1,0:T(8,128)} %copy-done.2, s32[1024]{0:T(1024)S(1)} %iota_add_fusion, f32[384]{0:T(512)S(1)} %log_add_fusion, s32[384]{0:T(512)} %param.11), kind=kOutput, calls=%fused_computation.13 | convolution fusion | flops 3632922624 | bytes 24013312 | tf_op jit(solution)/shard_map/dot_general | solution.py:70
  260.2 191.7 %all-reduce.4.cloned.1.call-done = f32[18432]{0:T(1024)} async-done(((f32[18432]{0:T(1024)}), f32[18432]{0:T(1024)}) %all-reduce.4.cloned.1.call-update) | async-done | bytes 73744
  453.4 147.6 %reduce-scatter.2.cloned.1.call-done = f32[144,1024]{1,0:T(8,128)} async-done(((f32[4608,1024]{1,0:T(8,128)}), f32[144,1024]{1,0:T(8,128)}) %reduce-scatter.2.cloned.1.call-update) | async-done | bytes 589840 | tf_op jit(solution)/shard_map/reduce_scatter | solution.py:69
  (80 shorter events, 43.7 us)
Async XLA Ops:
  7.2 77.8 %all-gather.5.cloned.1.call-start = ((), (), s32[]{:S(2)}) async-start(), calls=%async_computation.1 | async-start | bytes 3981312 | tf_op jit(solution)/shard_map/all_gather | solution.py:53
  7.9 444.0 %all-reduce.4.cloned.1.call-start = ((), (), s32[]{:S(2)}) async-start(), calls=%async_computation.3 | async-start | bytes 147456
  89.4 36.0 %slice-start = ((s8[9437184]{0:T(1024)(128)(4,1)}), s8[4194304]{0:T(1024)(128)(4,1)S(1)}, s32[]{:S(2)}) async-start(s8[9437184]{0:T(1024)(128)(4,1)} %bitcast.93), calls=%async_computation.4 | async-start | bytes 8388608
  90.2 35.2 %copy-start.5 = (s32[384]{0:T(512)S(1)}, s32[384]{0:T(512)}, u32[]{:S(2)}) copy-start(s32[384]{0:T(512)} %param.11) | copy-start | bytes 4612
  90.2 35.2 %slice-start.1 = ((s8[9437184]{0:T(1024)(128)(4,1)}), s8[4194304]{0:T(1024)(128)(4,1)S(1)}, s32[]{:S(2)}) async-start(s8[9437184]{0:T(1024)(128)(4,1)} %bitcast.93), calls=%async_computation.5 | async-start | bytes 8388608
  90.2 35.2 %slice-start.2 = ((s8[9437184]{0:T(1024)(128)(4,1)}), s8[1048576]{0:T(1024)(128)(4,1)S(1)}, s32[]{:S(2)}) async-start(s8[9437184]{0:T(1024)(128)(4,1)} %bitcast.93), calls=%async_computation.6 | async-start | bytes 2097152
  97.2 35.0 %copy-start.2 = (f32[384,1024]{1,0:T(8,128)}, f32[384,1024]{1,0:T(8,128)S(1)}, u32[]{:S(2)}) copy-start(f32[384,1024]{1,0:T(8,128)S(1)} %get-tuple-element.37) | copy-start | bytes 4718596
  144.7 8.1 %collective-permute-start.7 = (f32[288,384]{1,0:T(8,128)}, f32[288,384]{1,0:T(8,128)}, u32[]{:S(2)}, u32[]{:S(2)}) collective-permute-start(f32[288,384]{1,0:T(8,128)} %dynamic-slice_bitcast_fusion.1), channel_id=1, source_target_pairs={{0,4},{1,0},{2,1},{3,2},{7,3},{6,7},{5,6},{4,5},{8,12},{9,8},{10,9... | collective-permute-start | bytes 1327112 | tf_op jit(solution)/shard_map/ppermute | solution.py:43
  148.3 9.1 %collective-permute-start = (f32[296,384]{1,0:T(8,128)}, f32[296,384]{1,0:T(8,128)}, u32[]{:S(2)}, u32[]{:S(2)}) collective-permute-start(f32[296,384]{1,0:T(8,128)} %dynamic-slice_bitcast_fusion), channel_id=1, source_target_pairs={{0,1},{1,2},{2,3},{3,7},{7,6},{6,5},{5,4},{4,0},{8,9},{9,10},{10,1... | collective-permute-start | bytes 1363976 | tf_op jit(solution)/shard_map/ppermute | solution.py:42
  154.7 10.4 %collective-permute-start.8 = (f32[288,384]{1,0:T(8,128)}, f32[288,384]{1,0:T(8,128)}, u32[]{:S(2)}, u32[]{:S(2)}) collective-permute-start(f32[288,384]{1,0:T(8,128)} %bitcast_add_fusion.7), channel_id=1, source_target_pairs={{0,4},{1,0},{2,1},{3,2},{7,3},{6,7},{5,6},{4,5},{8,12},{9,8},{10,9... | collective-permute-start | bytes 1327112 | tf_op jit(solution)/shard_map/ppermute | solution.py:43
  159.4 10.8 %collective-permute-start.1 = (f32[296,384]{1,0:T(8,128)}, f32[296,384]{1,0:T(8,128)}, u32[]{:S(2)}, u32[]{:S(2)}) collective-permute-start(f32[296,384]{1,0:T(8,128)} %bitcast_add_fusion), channel_id=1, source_target_pairs={{0,1},{1,2},{2,3},{3,7},{7,6},{6,5},{5,4},{4,0},{8,9},{9,10},{10,1... | collective-permute-start | bytes 1363976 | tf_op jit(solution)/shard_map/ppermute | solution.py:42
  167.0 11.2 %collective-permute-start.9 = (f32[288,384]{1,0:T(8,128)}, f32[288,384]{1,0:T(8,128)}, u32[]{:S(2)}, u32[]{:S(2)}) collective-permute-start(f32[288,384]{1,0:T(8,128)} %bitcast_add_fusion.8), channel_id=1, source_target_pairs={{0,4},{1,0},{2,1},{3,2},{7,3},{6,7},{5,6},{4,5},{8,12},{9,8},{10,9... | collective-permute-start | bytes 1327112 | tf_op jit(solution)/shard_map/ppermute | solution.py:43
  172.2 11.9 %collective-permute-start.2 = (f32[296,384]{1,0:T(8,128)}, f32[296,384]{1,0:T(8,128)}, u32[]{:S(2)}, u32[]{:S(2)}) collective-permute-start(f32[296,384]{1,0:T(8,128)} %bitcast_add_fusion.1), channel_id=1, source_target_pairs={{0,1},{1,2},{2,3},{3,7},{7,6},{6,5},{5,4},{4,0},{8,9},{9,10},{10,1... | collective-permute-start | bytes 1363976 | tf_op jit(solution)/shard_map/ppermute | solution.py:42
  180.1 12.0 %collective-permute-start.10 = (f32[288,384]{1,0:T(8,128)}, f32[288,384]{1,0:T(8,128)}, u32[]{:S(2)}, u32[]{:S(2)}) collective-permute-start(f32[288,384]{1,0:T(8,128)} %bitcast_add_fusion.9), channel_id=1, source_target_pairs={{0,4},{1,0},{2,1},{3,2},{7,3},{6,7},{5,6},{4,5},{8,12},{9,8},{10,9... | collective-permute-start | bytes 1327112 | tf_op jit(solution)/shard_map/ppermute | solution.py:43
  186.0 13.0 %collective-permute-start.3 = (f32[296,384]{1,0:T(8,128)}, f32[296,384]{1,0:T(8,128)}, u32[]{:S(2)}, u32[]{:S(2)}) collective-permute-start(f32[296,384]{1,0:T(8,128)} %bitcast_add_fusion.2), channel_id=1, source_target_pairs={{0,1},{1,2},{2,3},{3,7},{7,6},{6,5},{5,4},{4,0},{8,9},{9,10},{10,1... | collective-permute-start | bytes 1363976 | tf_op jit(solution)/shard_map/ppermute | solution.py:42
  194.0 39.1 %copy-start.6 = (u32[256]{0:T(256)S(1)}, u32[256]{0:T(256)}, u32[]{:S(2)}) copy-start(u32[256]{0:T(256)} %constant.209) | copy-start | bytes 3076
  194.0 12.2 %collective-permute-start.11 = (f32[288,384]{1,0:T(8,128)}, f32[288,384]{1,0:T(8,128)}, u32[]{:S(2)}, u32[]{:S(2)}) collective-permute-start(f32[288,384]{1,0:T(8,128)} %bitcast_add_fusion.10), channel_id=1, source_target_pairs={{0,4},{1,0},{2,1},{3,2},{7,3},{6,7},{5,6},{4,5},{8,12},{9,8},{10,9... | collective-permute-start | bytes 1327112 | tf_op jit(solution)/shard_map/ppermute | solution.py:43
  201.0 14.1 %collective-permute-start.4 = (f32[296,384]{1,0:T(8,128)}, f32[296,384]{1,0:T(8,128)}, u32[]{:S(2)}, u32[]{:S(2)}) collective-permute-start(f32[296,384]{1,0:T(8,128)} %bitcast_add_fusion.3), channel_id=1, source_target_pairs={{0,1},{1,2},{2,3},{3,7},{7,6},{6,5},{5,4},{4,0},{8,9},{9,10},{10,1... | collective-permute-start | bytes 1363976 | tf_op jit(solution)/shard_map/ppermute | solution.py:42
  208.2 12.7 %collective-permute-start.12 = (f32[288,384]{1,0:T(8,128)}, f32[288,384]{1,0:T(8,128)}, u32[]{:S(2)}, u32[]{:S(2)}) collective-permute-start(f32[288,384]{1,0:T(8,128)} %bitcast_add_fusion.11), channel_id=1, source_target_pairs={{0,4},{1,0},{2,1},{3,2},{7,3},{6,7},{5,6},{4,5},{8,12},{9,8},{10,9... | collective-permute-start | bytes 1327112 | tf_op jit(solution)/shard_map/ppermute | solution.py:43
  217.1 13.3 %collective-permute-start.5 = (f32[296,384]{1,0:T(8,128)}, f32[296,384]{1,0:T(8,128)}, u32[]{:S(2)}, u32[]{:S(2)}) collective-permute-start(f32[296,384]{1,0:T(8,128)} %bitcast_add_fusion.4), channel_id=1, source_target_pairs={{0,1},{1,2},{2,3},{3,7},{7,6},{6,5},{5,4},{4,0},{8,9},{9,10},{10,1... | collective-permute-start | bytes 1363976 | tf_op jit(solution)/shard_map/ppermute | solution.py:42
  222.9 12.0 %collective-permute-start.13 = (f32[288,384]{1,0:T(8,128)}, f32[288,384]{1,0:T(8,128)}, u32[]{:S(2)}, u32[]{:S(2)}) collective-permute-start(f32[288,384]{1,0:T(8,128)} %bitcast_add_fusion.12), channel_id=1, source_target_pairs={{0,4},{1,0},{2,1},{3,2},{7,3},{6,7},{5,6},{4,5},{8,12},{9,8},{10,9... | collective-permute-start | bytes 1327112 | tf_op jit(solution)/shard_map/ppermute | solution.py:43
  232.3 12.4 %collective-permute-start.6 = (f32[296,384]{1,0:T(8,128)}, f32[296,384]{1,0:T(8,128)}, u32[]{:S(2)}, u32[]{:S(2)}) collective-permute-start(f32[296,384]{1,0:T(8,128)} %bitcast_add_fusion.5), channel_id=1, source_target_pairs={{0,1},{1,2},{2,3},{3,7},{7,6},{6,5},{5,4},{4,0},{8,9},{9,10},{10,1... | collective-permute-start | bytes 1363976 | tf_op jit(solution)/shard_map/ppermute | solution.py:42
  232.3 13.6 %copy-start.3 = (bf16[384,576]{0,1:T(8,128)(2,1)S(1)}, bf16[384,576]{0,1:T(8,128)(2,1)}, u32[]{:S(2)}) copy-start(bf16[384,576]{0,1:T(8,128)(2,1)} %param.8) | copy-start | bytes 1327108
  249.2 351.8 %reduce-scatter.2.cloned.1.call-start = ((), (), s32[]{:S(2)}) async-start(), calls=%async_computation.2 | async-start | bytes 19464192 | tf_op jit(solution)/shard_map/reduce_scatter | solution.py:69
  (3 other events, 4.6 us)
Sparse Core Ops, SparseCore 0:
  10.6 74.3 all-gather.4
  249.3 202.5 all-reduce.3
  455.2 145.7 reduce-scatter.1
